TPU v7x, 256 devices: a whole 4x4x8 slice. The times are simulated.
256 devices in a mesh: expert: 64 (over z, y, x_hi), tensor: 4 (over x_lo, core).
Axes of the slice: x: 4 (x_hi: 2, x_lo: 2; x = x_hi * 2 + x_lo), y: 4, z: 8, core: 2. Of those that a mesh axis runs over, the one named last changes fastest.
Arguments:
- attn_partial: bfloat16 [4, 8192, 4096], P('tensor', 'expert'), may hold values from -4 to 4
- residual: bfloat16 [8192, 4096], P('expert', 'tensor'), may hold values from -40 to 40
- norm_gain: float32 [4096], P('tensor'), may hold values from 0.1 to 1.9
- expert_ids: int32 [8192, 4], P('expert'), may hold values from 0 to 63, all different within a row; in each aligned block of 128 rows (0 to 127, 128 to 255, ...) at most 10 rows name the same one
- route_weight: float32 [8192, 4], P('expert'), may hold values from 0.1 to 1
- w_in: bfloat16 [64, 4096, 2048], P('expert', 'tensor'), may hold values from -0.09375 to 0.09375
- w_down: bfloat16 [64, 1024, 4096], P('expert', None, 'tensor'), may hold values from -0.1875 to 0.1875
Outputs:
- layer_out: bfloat16 [8192, 4096], P('expert', 'tensor')
Inputs may be any that keep to these rules, and one draw needn't show every extreme that they name: `expert_ids`: in each aligned block of 128 rows (the tokens of one index of expert) no expert is named by more than 10 rows, a bound that some block reaches. A row names 4 different experts.
All inputs are finite; a program needn't handle non-finite values.
Results may differ from a plain program's by a relative error of at most 0.01.
Values may be sent and summed in bfloat16 or wider, within the bound.
No kernel may reach another device: no remote copies, remote signals or barrier semaphores. Data moves between devices by JAX's collectives and lax.ppermute only.
A program may use at most 64 MiB of HBM per device.

v0:
```python
import jax
import jax.numpy as jnp
from jax import lax
from jax.sharding import PartitionSpec as P


def body(attn_partial, residual, norm_gain, expert_ids, route_weight, w_in, w_down):
    token_count = expert_ids.shape[0]
    topk_count = expert_ids.shape[1]
    feature_local = residual.shape[1]
    feature_count = feature_local * lax.axis_size("tensor")
    hidden_width = w_down.shape[1]
    expert_count = lax.axis_size("expert")
    capacity = 5 * token_count * topk_count // (4 * expert_count)
    attention = lax.psum_scatter(
        attn_partial[0].astype(jnp.float32).astype(jnp.bfloat16),
        "tensor",
        scatter_dimension=1,
        tiled=True,
    ).astype(jnp.float32)
    stream = residual.astype(jnp.float32) + attention
    squares = lax.psum(jnp.sum(stream * stream, axis=1), "tensor")
    inverse = lax.rsqrt(squares / feature_count + 1e-06)[:, None]
    normed = stream * inverse * norm_gain[None, :]
    rows = normed.astype(jnp.bfloat16)
    flat_ids = expert_ids.reshape(-1)
    one_hot = (flat_ids[:, None] == jnp.arange(expert_count, dtype=jnp.int32)[None, :]).astype(
        jnp.int32
    )
    earlier = jnp.cumsum(one_hot, axis=0) - one_hot
    slot_index = jnp.sum(earlier * one_hot, axis=1)
    positions = (flat_ids * capacity + slot_index).reshape(token_count, topk_count)
    places = jnp.arange(expert_count * capacity, dtype=jnp.int32)
    matches = positions[None, :, :] == places[:, None, None]
    dispatch = jnp.any(matches, axis=2)
    sent_rows = jnp.dot(dispatch.astype(jnp.bfloat16), rows, preferred_element_type=jnp.float32)
    sent_rows = sent_rows.astype(jnp.bfloat16).reshape(expert_count, capacity, feature_local)
    weights_table = jnp.sum(jnp.where(matches, route_weight[None, :, :], 0.0), axis=2).T
    in_rows = lax.all_to_all(sent_rows, "expert", split_axis=0, concat_axis=0, tiled=True)
    source_count = in_rows.shape[0]
    item_count = in_rows.shape[1]
    row_total = source_count * item_count
    flat_rows = in_rows.reshape(row_total, feature_local)
    partial_value = jnp.dot(flat_rows, w_in[0], preferred_element_type=jnp.float32)
    total = lax.psum_scatter(
        partial_value.astype(jnp.bfloat16), "tensor", scatter_dimension=0, tiled=True
    ).astype(jnp.float32)
    hidden = (jax.nn.silu(total[:, :hidden_width]) * total[:, hidden_width:]).astype(jnp.bfloat16)
    hidden = lax.all_gather(hidden, "tensor", axis=0, tiled=True)
    produced = jnp.dot(hidden, w_down[0], preferred_element_type=jnp.float32).astype(jnp.bfloat16)
    results = produced.reshape(source_count, item_count, feature_local)
    returned = lax.all_to_all(results, "expert", split_axis=0, concat_axis=0, tiled=True)
    routed = jnp.dot(
        weights_table,
        returned.reshape(expert_count * capacity, feature_local).astype(jnp.float32),
        precision=lax.Precision.HIGHEST,
    )
    return (stream + routed).astype(jnp.bfloat16)


def solution(mesh):
    in_specs = (
        P("tensor", "expert", None),
        P("expert", "tensor"),
        P("tensor"),
        P("expert", None),
        P("expert", None),
        P("expert", "tensor", None),
        P("expert", None, "tensor"),
    )
    out_specs = P("expert", "tensor")
    return jax.shard_map(body, mesh=mesh, in_specs=in_specs, out_specs=out_specs, check_vma=False)
```

profile of v0, /device:TPU:32, one launch (start us, length us, event | category | flops | bytes accessed | tf_op | source)
XLA Modules:
  0.0 259.2 jit_solution(11429051957058724072)
XLA Ops:
  6.5 0.0 copy-start
  6.5 0.0 copy-start.2
  6.5 0.0 copy-start.1
  6.5 0.0 reduce-scatter.3.cloned.1.call-start
  6.5 0.0 copy-start.3
  6.6 0.7 reduce-scatter.3.cloned.1.call-update
  7.3 0.0 reduce-scatter.5.cloned.1.call-start
  7.3 0.8 copy.22
  8.1 0.1 eq.42
  8.2 0.1 eq.38
  8.3 1.2 reduce-window.6
  9.5 0.2 slice_reduce_fusion
  9.8 0.1 fusion.17
  9.9 0.1 reduce_sum.30
  10.1 0.1 copy.25
  10.1 0.0 copy-done.2
  10.1 0.2 fusion.10
  10.3 24.9 %reduce-scatter.3.cloned.1.call-done = bf16[128,1024]{1,0:T(8,128)(2,1)} async-done(((bf16[128,4096]{1,0:T(8,128)(2,1)}), bf16[128,1024]{1,0:T(8,128)(2,1)}) %reduce-scatter.3.cloned.1.call-update) | async-done | bytes 262160 | tf_op jit(solution)/shard_map/reduce_scatter | solution.py:15
  35.2 0.0 copy-done.1
  35.2 1.1 multiply_reduce_fusion
  36.4 6.4 %psum.7 = f32[128]{0:T(128)S(1)} all-reduce(f32[128]{0:T(128)S(1)} %multiply_reduce_fusion), channel_id=1, replica_groups=mesh['expert'=64,'tensor'=4] {'tensor'}, use_global_device_ids=true, to_apply=%region_7.8 | all-reduce | flops 128 | bytes 1024 | tf_op jit(solution)/shard_map/psum | solution.py:22
  42.8 0.0 copy-done.3
  42.8 1.6 convolution_convert_fusion
  44.4 1.6 reshape.40
  46.0 64.5 %all_to_all.10 = bf16[64,10,1024]{2,1,0:T(8,128)(2,1)} all-to-all(bf16[64,10,1024]{2,1,0:T(8,128)(2,1)} %reshape.40), channel_id=1, replica_groups=mesh['expert'=64,'tensor'=4] {'expert'}, dimensions={0} | all-to-all | bytes 2621440 | tf_op jit(solution)/shard_map/all_to_all | solution.py:39
  110.5 2.6 reshape.41
  113.0 6.3 %fusion.2 = bf16[640,2048]{1,0:T(8,128)(2,1)} fusion(bf16[640,1024]{1,0:T(8,128)(2,1)S(1)} %reshape.41, bf16[1,1024,2048]{2,1,0:T(8,128)(2,1)} %param.12), kind=kOutput, calls=%fused_computation.2 | convolution fusion | flops 2685665280 | bytes 8126464 | tf_op jit(solution)/shard_map/dot_general | solution.py:44
  119.4 0.0 reduce-scatter.5.cloned.1.call-update
  119.4 0.0 all-gather.2.cloned.1.call-start
  119.5 29.7 %reduce-scatter.5.cloned.1.call-done = bf16[160,2048]{1,0:T(8,128)(2,1)} async-done(((bf16[640,2048]{1,0:T(8,128)(2,1)}), bf16[160,2048]{1,0:T(8,128)(2,1)}) %reduce-scatter.5.cloned.1.call-update) | async-done | bytes 655376 | tf_op jit(solution)/shard_map/reduce_scatter | solution.py:45
  149.1 1.2 convert_element_type.45
  150.4 0.9 fusion.12
  151.3 0.0 all-gather.2.cloned.1.call-update
  151.3 26.1 %all-gather.2.cloned.1.call-done = bf16[640,1024]{1,0:T(8,128)(2,1)} async-done(((bf16[160,1024]{1,0:T(8,128)(2,1)}), bf16[640,1024]{1,0:T(8,128)(2,1)}) %all-gather.2.cloned.1.call-update) | async-done | bytes 1310736 | tf_op jit(solution)/shard_map/all_gather | solution.py:49
  177.5 0.0 copy-done
  177.5 2.8 %fusion.7 = bf16[640,1024]{1,0:T(8,128)(2,1)S(1)} fusion(bf16[640,1024]{1,0:T(8,128)(2,1)} %all-gather.2.cloned.1.call-done, bf16[1,1024,1024]{2,1,0:T(8,128)(2,1)S(1)} %copy-done), kind=kOutput, calls=%fused_computation.5 | convolution fusion | flops 1342832640 | bytes 4718592 | tf_op jit(solution)/shard_map/dot_general | solution.py:50
  180.3 1.5 reshape.42
  181.8 0.0 copy-start.4
  181.8 12.9 %all-to-all-start.1 = ((bf16[64,10,1024]{2,1,0:T(8,128)(2,1)}), bf16[64,10,1024]{2,1,0:T(8,128)(2,1)}, u32[]{:S(2)}, u32[]{:S(2)}) async-start(bf16[64,10,1024]{2,1,0:T(8,128)(2,1)} %reshape.42), calls=%async_computation.3 | async-start | bytes 4194304 | tf_op jit(solution)/shard_map/all_to_all | solution.py:52
  194.8 0.0 copy-done.4
  194.8 0.9 select_reduce_fusion
  195.6 51.7 %all-to-all-done.1 = bf16[64,10,1024]{2,1,0:T(8,128)(2,1)} async-done(((bf16[64,10,1024]{2,1,0:T(8,128)(2,1)}), bf16[64,10,1024]{2,1,0:T(8,128)(2,1)}, u32[]{:S(2)}, u32[]{:S(2)}) %all-to-all-start.1) | async-done | bytes 1310752 | tf_op jit(solution)/shard_map/all_to_all | solution.py:52
  247.4 2.6 reshape.43
  250.0 2.7 %fusion.11 = bf16[128,1024]{1,0:T(8,128)(2,1)} fusion(f32[640,128]{1,0:T(8,128)} %select_reduce_fusion, bf16[640,1024]{1,0:T(8,128)(2,1)S(1)} %reshape.43, bf16[128,1024]{1,0:T(8,128)(2,1)} %reduce-scatter.3.cloned.1.call-done, bf16[128,1024]{1,0:T(8,128)(2,1)} %param.8), kind=kOutput, calls=%fused_computation.11 | convolution fusion | flops 1007288320 | bytes 2424832 | tf_op jit(solution)/shard_map/dot_general | solution.py:53
  (5 shorter events, 0.1 us)
Async XLA Ops:
  6.5 170.9 %copy-start = (bf16[1,1024,1024]{2,1,0:T(8,128)(2,1)S(1)}, bf16[1,1024,1024]{2,1,0:T(8,128)(2,1)}, u32[]{:S(2)}) copy-start(bf16[1,1024,1024]{2,1,0:T(8,128)(2,1)} %param.13) | copy-start | bytes 6291460
  6.5 3.6 %copy-start.2 = (s32[128,4]{0,1:T(4,128)S(1)}, s32[128,4]{0,1:T(4,128)}, u32[]{:S(2)}) copy-start(s32[128,4]{0,1:T(4,128)} %param.10) | copy-start | bytes 6148
  6.5 28.7 %copy-start.1 = (bf16[128,1024]{1,0:T(8,128)(2,1)S(1)}, bf16[128,1024]{1,0:T(8,128)(2,1)}, u32[]{:S(2)}) copy-start(bf16[128,1024]{1,0:T(8,128)(2,1)} %param.8) | copy-start | bytes 786436
  6.5 28.7 %reduce-scatter.3.cloned.1.call-start = ((), (), s32[]{:S(2)}) async-start(), calls=%async_computation.4 | async-start | bytes 1310720 | tf_op jit(solution)/shard_map/reduce_scatter | solution.py:15
  6.5 36.2 %copy-start.3 = (f32[1024]{0:T(1024)S(1)}, f32[1024]{0:T(1024)}, u32[]{:S(2)}) copy-start(f32[1024]{0:T(1024)} %param.9) | copy-start | bytes 12292
  7.3 141.9 %reduce-scatter.5.cloned.1.call-start = ((), (), s32[]{:S(2)}) async-start(), calls=%async_computation.5 | async-start | bytes 3276800 | tf_op jit(solution)/shard_map/reduce_scatter | solution.py:45
  119.4 58.0 %all-gather.2.cloned.1.call-start = ((), (), s32[]{:S(2)}) async-start(), calls=%async_computation.6 | async-start | bytes 1638400 | tf_op jit(solution)/shard_map/all_gather | solution.py:49
  181.8 12.9 %copy-start.4 = (f32[128,4]{0,1:T(4,128)S(1)}, f32[128,4]{0,1:T(4,128)}, u32[]{:S(2)}) copy-start(f32[128,4]{0,1:T(4,128)} %param.11) | copy-start | bytes 6148
  181.8 65.6 %all-to-all-start.1 = ((bf16[64,10,1024]{2,1,0:T(8,128)(2,1)}), bf16[64,10,1024]{2,1,0:T(8,128)(2,1)}, u32[]{:S(2)}, u32[]{:S(2)}) async-start(bf16[64,10,1024]{2,1,0:T(8,128)(2,1)} %reshape.42), calls=%async_computation.3 | async-start | bytes 4194304 | tf_op jit(solution)/shard_map/all_to_all | solution.py:52
Sparse Core Ops, SparseCore 0:
  9.9 25.3 reduce-scatter.2
  119.5 29.5 reduce-scatter.4
  151.5 25.9 all-gather.1
where the time goes:
time: 260 us; the launch traced here: 259 us
  waiting for transfers between devices  133 us (51%)
  blocking collectives  70.9 us (27%)
  matrix products  13.5 us (5%)
  between operations  13.2 us (5%)
  starting transfers between devices  13 us (5%)
  local copies, waits for them, and re-layouts  9.65 us (4%)
  other arithmetic  5.72 us (2%)
    all_to_all x1, blocking collectives, body(): lax.all_to_all(sent_rows, 'expert', split_axis=0, concat_axis=0, tiled=True)  64.5 us
    all_to_all x1, waiting for transfers between devices, body(): lax.all_to_all(results, 'expert', split_axis=0, concat_axis=0, tiled=True)  51.7 us
    reduce_scatter x1, waiting for transfers between devices, body(): lax.psum_scatter(partial_value.astype(jnp.bfloat16), 'tensor', scatter_di...  29.7 us
    all_gather x1, waiting for transfers between devices, body(): hidden = lax.all_gather(hidden, 'tensor', axis=0, tiled=True)  26.1 us
    reduce_scatter x1, waiting for transfers between devices, body(): lax.psum_scatter(attn_partial[0].astype(jnp.float32).astype(jnp.bfloat16)...  24.9 us
    all_to_all x1, starting transfers between devices, body(): lax.all_to_all(results, 'expert', split_axis=0, concat_axis=0, tiled=True)  12.9 us
    psum x1, blocking collectives, body(): squares = lax.psum(jnp.sum(stream * stream, axis=1), 'tensor')  6.38 us
    dot_general x1, matrix products, body(): jnp.dot(flat_rows, w_in[0], preferred_element_type=jnp.float32)  6.35 us
  transfers between devices with their start and end apart: 4, of which 4 were waited for; matrix products, arithmetic and copies ran while one was open for 1% of the time, Pallas kernels for 0%

commit v1 on v0

--- a/solution.py
+++ b/solution.py
@@ -46,7 +46,9 @@
         partial_value.astype(jnp.bfloat16), "tensor", scatter_dimension=0, tiled=True
     ).astype(jnp.float32)
     hidden = (jax.nn.silu(total[:, :hidden_width]) * total[:, hidden_width:]).astype(jnp.bfloat16)
-    hidden = lax.all_gather(hidden, "tensor", axis=0, tiled=True)
+    hidden = jnp.concatenate(
+        lax.all_to_all(jnp.stack([hidden] * lax.axis_size("tensor")), "tensor", 0, 0), axis=0
+    )
     produced = jnp.dot(hidden, w_down[0], preferred_element_type=jnp.float32).astype(jnp.bfloat16)
     results = produced.reshape(source_count, item_count, feature_local)
     returned = lax.all_to_all(results, "expert", split_axis=0, concat_axis=0, tiled=True)

time: 260 us -> 251 us (0.965)
  waiting for transfers between devices: 133 us -> 106 us
  blocking collectives: 70.9 us -> 90.6 us
    all_gather x1 -> x0, waiting for transfers between devices: 26.1 us -> none  [body(): hidden = lax.all_gather(hidden, 'tensor', axis=0, tiled=True)]
    all_to_all x0 -> x1, blocking collectives: none -> 19.7 us  [body(): lax.all_to_all(jnp.stack([hidden] * lax.axis_size('tensor')), 'tensor', 0...]
  transfers between devices with their start and end apart: 4 -> 3, of which waited for: 4 -> 3; matrix products, arithmetic and copies ran while one was open for 1% -> 2% of each run, Pallas kernels for 0% -> 0%
where the time goes in v1:
time: 251 us; the launch traced here: 250 us
  waiting for transfers between devices  106 us (42%)
  blocking collectives  90.6 us (36%)
  between operations  13.5 us (5%)
  starting transfers between devices  13 us (5%)
  matrix products  12.2 us (5%)
  local copies, waits for them, and re-layouts  9.81 us (4%)
  other arithmetic  4.96 us (2%)
    all_to_all x1, blocking collectives, body(): lax.all_to_all(sent_rows, 'expert', split_axis=0, concat_axis=0, tiled=True)  64.5 us
    all_to_all x1, waiting for transfers between devices, body(): lax.all_to_all(results, 'expert', split_axis=0, concat_axis=0, tiled=True)  50.5 us
    reduce_scatter x1, waiting for transfers between devices, body(): lax.psum_scatter(partial_value.astype(jnp.bfloat16), 'tensor', scatter_di...  29.7 us
    reduce_scatter x1, waiting for transfers between devices, body(): lax.psum_scatter(attn_partial[0].astype(jnp.float32).astype(jnp.bfloat16)...  24.9 us
    all_to_all x1, blocking collectives, body(): lax.all_to_all(jnp.stack([hidden] * lax.axis_size('tensor')), 'tensor', 0...  19.7 us
    all_to_all x1, starting transfers between devices, body(): lax.all_to_all(results, 'expert', split_axis=0, concat_axis=0, tiled=True)  12.9 us
    psum x1, blocking collectives, body(): squares = lax.psum(jnp.sum(stream * stream, axis=1), 'tensor')  6.38 us
    dot_general x1, matrix products, body(): jnp.dot(flat_rows, w_in[0], preferred_element_type=jnp.float32)  6.35 us
  transfers between devices with their start and end apart: 3, of which 3 were waited for; matrix products, arithmetic and copies ran while one was open for 2% of the time, Pallas kernels for 0%

profile of v1, /device:TPU:32, one launch (start us, length us, event | category | flops | bytes accessed | tf_op | source)
XLA Modules:
  0.0 249.9 jit_solution(17327919110416782305)
XLA Ops:
  6.5 0.0 copy-start
  6.5 0.0 copy-start.2
  6.5 0.0 copy-start.1
  6.5 0.0 reduce-scatter.3.cloned.1.call-start
  6.5 0.0 copy-start.3
  6.6 0.7 reduce-scatter.3.cloned.1.call-update
  7.3 0.0 reduce-scatter.5.cloned.1.call-start
  7.3 0.8 copy.22
  8.1 0.1 eq.42
  8.2 0.1 eq.38
  8.3 1.2 reduce-window.6
  9.5 0.2 slice_reduce_fusion
  9.8 0.1 fusion.17
  9.9 0.1 reduce_sum.30
  10.1 0.1 copy.25
  10.1 0.0 copy-done.2
  10.1 0.2 fusion.10
  10.3 24.9 %reduce-scatter.3.cloned.1.call-done = bf16[128,1024]{1,0:T(8,128)(2,1)} async-done(((bf16[128,4096]{1,0:T(8,128)(2,1)}), bf16[128,1024]{1,0:T(8,128)(2,1)}) %reduce-scatter.3.cloned.1.call-update) | async-done | bytes 262160 | tf_op jit(solution)/shard_map/reduce_scatter | solution.py:15
  35.2 0.0 copy-done.1
  35.2 1.1 multiply_reduce_fusion
  36.4 6.4 %psum.7 = f32[128]{0:T(128)S(1)} all-reduce(f32[128]{0:T(128)S(1)} %multiply_reduce_fusion), channel_id=1, replica_groups=mesh['expert'=64,'tensor'=4] {'tensor'}, use_global_device_ids=true, to_apply=%region_7.8 | all-reduce | flops 128 | bytes 1024 | tf_op jit(solution)/shard_map/psum | solution.py:22
  42.8 0.0 copy-done.3
  42.8 1.6 convolution_convert_fusion
  44.4 1.6 reshape.45
  46.0 64.5 %all_to_all.15 = bf16[64,10,1024]{2,1,0:T(8,128)(2,1)} all-to-all(bf16[64,10,1024]{2,1,0:T(8,128)(2,1)} %reshape.45), channel_id=1, replica_groups=mesh['expert'=64,'tensor'=4] {'expert'}, dimensions={0} | all-to-all | bytes 2621440 | tf_op jit(solution)/shard_map/all_to_all | solution.py:39
  110.5 2.6 %reshape.46 = bf16[640,1024]{1,0:T(8,128)(2,1)S(1)} reshape(bf16[64,10,1024]{2,1,0:T(8,128)(2,1)} %all_to_all.15) | data formatting | bytes 2621440 | tf_op jit(solution)/shard_map/reshape | solution.py:43
  113.0 6.3 %fusion.2 = bf16[640,2048]{1,0:T(8,128)(2,1)} fusion(bf16[640,1024]{1,0:T(8,128)(2,1)S(1)} %reshape.46, bf16[1,1024,2048]{2,1,0:T(8,128)(2,1)} %param.12), kind=kOutput, calls=%fused_computation.2 | convolution fusion | flops 2685665280 | bytes 8126464 | tf_op jit(solution)/shard_map/dot_general | solution.py:44
  119.4 0.0 reduce-scatter.5.cloned.1.call-update
  119.4 29.7 %reduce-scatter.5.cloned.1.call-done = bf16[160,2048]{1,0:T(8,128)(2,1)} async-done(((bf16[640,2048]{1,0:T(8,128)(2,1)}), bf16[160,2048]{1,0:T(8,128)(2,1)}) %reduce-scatter.5.cloned.1.call-update) | async-done | bytes 655376 | tf_op jit(solution)/shard_map/reduce_scatter | solution.py:45
  149.1 1.2 convert_element_type.45
  150.4 0.2 fusion.12
  150.6 0.2 stack.2
  150.7 19.7 %all_to_all.16 = bf16[4,160,1024]{2,1,0:T(8,128)(2,1)S(1)} all-to-all(bf16[4,160,1024]{2,1,0:T(8,128)(2,1)S(1)} %stack.2), channel_id=1, replica_groups=mesh['expert'=64,'tensor'=4] {'tensor'}, dimensions={0} | all-to-all | bytes 2621440 | tf_op jit(solution)/shard_map/all_to_all | solution.py:50
  170.4 0.0 copy-done
  170.4 1.5 fusion.7
  172.0 1.5 reshape.48
  173.5 0.0 copy-start.4
  173.5 12.9 %all-to-all-start.2 = ((bf16[64,10,1024]{2,1,0:T(8,128)(2,1)}), bf16[64,10,1024]{2,1,0:T(8,128)(2,1)}, u32[]{:S(2)}, u32[]{:S(2)}) async-start(bf16[64,10,1024]{2,1,0:T(8,128)(2,1)} %reshape.48), calls=%async_computation.4 | async-start | bytes 4194304 | tf_op jit(solution)/shard_map/all_to_all | solution.py:54
  186.4 0.0 copy-done.4
  186.4 0.9 select_reduce_fusion
  187.3 50.5 %all-to-all-done.2 = bf16[64,10,1024]{2,1,0:T(8,128)(2,1)} async-done(((bf16[64,10,1024]{2,1,0:T(8,128)(2,1)}), bf16[64,10,1024]{2,1,0:T(8,128)(2,1)}, u32[]{:S(2)}, u32[]{:S(2)}) %all-to-all-start.2) | async-done | bytes 1310752 | tf_op jit(solution)/shard_map/all_to_all | solution.py:54
  237.8 2.6 %reshape.49 = bf16[640,1024]{1,0:T(8,128)(2,1)S(1)} reshape(bf16[64,10,1024]{2,1,0:T(8,128)(2,1)} %all-to-all-done.2) | data formatting | bytes 2621440 | tf_op jit(solution)/shard_map/reshape | solution.py:57
  240.4 2.7 %fusion.11 = bf16[128,1024]{1,0:T(8,128)(2,1)} fusion(f32[640,128]{1,0:T(8,128)} %select_reduce_fusion, bf16[640,1024]{1,0:T(8,128)(2,1)S(1)} %reshape.49, bf16[128,1024]{1,0:T(8,128)(2,1)} %reduce-scatter.3.cloned.1.call-done, bf16[128,1024]{1,0:T(8,128)(2,1)} %param.8), kind=kOutput, calls=%fused_computation.11 | convolution fusion | flops 1007288320 | bytes 2424832 | tf_op jit(solution)/shard_map/dot_general | solution.py:55
  (5 shorter events, 0.1 us)
Async XLA Ops:
  6.5 163.9 %copy-start = (bf16[1,1024,1024]{2,1,0:T(8,128)(2,1)S(1)}, bf16[1,1024,1024]{2,1,0:T(8,128)(2,1)}, u32[]{:S(2)}) copy-start(bf16[1,1024,1024]{2,1,0:T(8,128)(2,1)} %param.13) | copy-start | bytes 6291460
  6.5 3.6 %copy-start.2 = (s32[128,4]{0,1:T(4,128)S(1)}, s32[128,4]{0,1:T(4,128)}, u32[]{:S(2)}) copy-start(s32[128,4]{0,1:T(4,128)} %param.10) | copy-start | bytes 6148
  6.5 28.7 %copy-start.1 = (bf16[128,1024]{1,0:T(8,128)(2,1)S(1)}, bf16[128,1024]{1,0:T(8,128)(2,1)}, u32[]{:S(2)}) copy-start(bf16[128,1024]{1,0:T(8,128)(2,1)} %param.8) | copy-start | bytes 786436
  6.5 28.7 %reduce-scatter.3.cloned.1.call-start = ((), (), s32[]{:S(2)}) async-start(), calls=%async_computation.5 | async-start | bytes 1310720 | tf_op jit(solution)/shard_map/reduce_scatter | solution.py:15
  6.5 36.2 %copy-start.3 = (f32[1024]{0:T(1024)S(1)}, f32[1024]{0:T(1024)}, u32[]{:S(2)}) copy-start(f32[1024]{0:T(1024)} %param.9) | copy-start | bytes 12292
  7.3 141.9 %reduce-scatter.5.cloned.1.call-start = ((), (), s32[]{:S(2)}) async-start(), calls=%async_computation.6 | async-start | bytes 3276800 | tf_op jit(solution)/shard_map/reduce_scatter | solution.py:45
  173.5 12.9 %copy-start.4 = (f32[128,4]{0,1:T(4,128)S(1)}, f32[128,4]{0,1:T(4,128)}, u32[]{:S(2)}) copy-start(f32[128,4]{0,1:T(4,128)} %param.11) | copy-start | bytes 6148
  173.5 64.3 %all-to-all-start.2 = ((bf16[64,10,1024]{2,1,0:T(8,128)(2,1)}), bf16[64,10,1024]{2,1,0:T(8,128)(2,1)}, u32[]{:S(2)}, u32[]{:S(2)}) async-start(bf16[64,10,1024]{2,1,0:T(8,128)(2,1)} %reshape.48), calls=%async_computation.4 | async-start | bytes 4194304 | tf_op jit(solution)/shard_map/all_to_all | solution.py:54
Sparse Core Ops, SparseCore 0:
  9.9 25.3 reduce-scatter.2
  119.5 29.5 reduce-scatter.4
